TPU v7x, 256 devices: a whole 4x4x8 slice. The times are simulated.
256 devices in a mesh: req: 32 (over z, x), tp: 8 (over y, core).
Axes of the slice: x: 4, y: 4, z: 8, core: 2. Of those that a mesh axis runs over, the one named last changes fastest.
Arguments:
- hidden: bfloat16 [8192, 2048], P('req'), may hold values from -6 to 6
- kv_cache: bfloat16 [2, 1024, 128, 2048], P(None, 'req', None, 'tp'), may hold values from -64 to 64
- page_table: int32 [128, 8], P('req'), may hold values from 0 to 31, as said below
- cache_lens: int32 [128], P('req'), may hold values from 1 to 1024
- parents: int32 [128, 64], P('req'), may hold values from 0 to 62, as said below
- accepted: int32 [128, 8], P('req'), may hold values from 0 to 14, as said below
- attn_gain: float32 [2048], replicated, may hold values from 0.1 to 1.9
- w_qkv: bfloat16 [2048, 3, 2048], P(None, None, 'tp'), may hold values from -0.125 to 0.125
- qk_gain: float32 [2, 2048], P(None, 'tp'), may hold values from 0.5 to 8
- w_out: bfloat16 [2048, 2048], P('tp'), may hold values from -0.5 to 0.5
- moe_gain: float32 [2048], replicated, may hold values from 0.1 to 1.9
- routes: int32 [8192, 8], P('req'), may hold values from 0 to 63, all different within a row; in each aligned block of 256 rows (0 to 255, 256 to 511, ...) at most 40 rows name the same one
- route_weights: float32 [8192, 8], P('req'), may hold values from 0.1 to 1
- w_gate_up: bfloat16 [32, 2048, 2, 2048], P('req', None, None, 'tp'), may hold values from -0.125 to 0.125
- w_down: bfloat16 [32, 2048, 2048], P('req', 'tp'), may hold values from -0.1875 to 0.1875
Outputs:
- output: bfloat16 [8192, 2048], P('req', 'tp')
- accepted_kv: bfloat16 [2, 1024, 2048], P(None, 'req', 'tp')
Inputs may be any that keep to these rules, and one draw needn't show every extreme that they name: `page_table`: values lie in the block of 32 pages of the request's group of 4 requests; within a group every page is used once. parents[r, 0] = 0 and parents[r, j] < j for j >= 1. accepted[r] are the first 8 slots, from the root down, of a path in request r's tree. `routes`: in each aligned block of 256 rows (the tokens of one index of req), no expert is named by more than 40 rows.
All inputs are finite; a program needn't handle non-finite values.
Results may differ from a plain program's by a relative error of at most 0.012.
The roundings to bfloat16 on the way count: a program that leaves them out, or rounds other values in their place, can miss the bound.
Values may be sent and summed in bfloat16 or wider, within the bound.
No kernel may reach another device: no remote copies, remote signals or barrier semaphores. Data moves between devices by JAX's collectives and lax.ppermute only.
A program may use at most 128 MiB of HBM per device.

v0:
```python
import jax
import jax.numpy as jnp
from jax import lax
from jax.sharding import Mesh, PartitionSpec as P

HD = 128
FFE = 1024
EXPERTS = 64
CAP = 40
TP = ("th", "tl", "tc")
norm_eps = 1e-05
rope_base = 10000.0
masked_score = -1e30


def rms_scale(values, gain):
    return values * lax.rsqrt(jnp.mean(values * values, axis=-1, keepdims=True) + norm_eps) * gain


def tree_masks(parents):
    slot_count = parents.shape[-1]
    slot_ids = jnp.arange(slot_count, dtype=jnp.int32)
    parent_hot = (parents[..., :, None] == slot_ids).astype(jnp.float32)
    ancestry = jnp.minimum(jnp.eye(slot_count, dtype=jnp.float32) + parent_hot, 1.0)
    for squaring in range(slot_count.bit_length()):
        ancestry = jnp.minimum(
            jnp.einsum("rij,rjk->rik", ancestry, ancestry, precision=lax.Precision.HIGHEST), 1.0
        )
    depths = jnp.sum(ancestry, axis=-1).astype(jnp.int32) - 1
    return (ancestry, depths)


def rotate(values, positions):
    head_dim = values.shape[-1]
    half_dim = head_dim // 2
    frequency = rope_base ** (-jnp.arange(half_dim, dtype=jnp.float32) * 2.0 / head_dim)
    angles = positions.astype(jnp.float32)[:, None] * frequency[None, :]
    cosine = jnp.cos(angles)[:, None, :]
    sine_part = jnp.sin(angles)[:, None, :]
    first_half = values[..., :half_dim]
    second = values[..., half_dim:]
    return jnp.concatenate(
        [first_half * cosine - second * sine_part, second * cosine + first_half * sine_part],
        axis=-1,
    )


def local(
    hidden,
    kv_cache,
    page_table,
    cache_lens,
    parents,
    accepted,
    attn_gain,
    w_qkv,
    qk_gain,
    w_out,
    moe_gain,
    routes,
    route_weights,
    w_gate_up,
    w_down,
):
    tok_rows, model_width = hidden.shape
    th = lax.axis_index("th")
    tl = lax.axis_index("tl")
    tc = lax.axis_index("tc")
    tp_count = lax.axis_size(TP)
    req_count = lax.axis_size("req")
    slice_width = model_width // tp_count
    slice_start = ((th * lax.axis_size("tl") + tl) * lax.axis_size("tc") + tc) * slice_width
    req_local, draft_len = parents.shape
    feat_dev = w_qkv.shape[2]
    local_heads = feat_dev // HD
    ancestry, depths = tree_masks(parents)
    positions = (cache_lens[:, None] + depths).reshape(-1)
    normed_in = rms_scale(hidden.astype(jnp.float32), attn_gain).astype(jnp.bfloat16)
    projected = jnp.dot(
        normed_in, w_qkv.reshape(model_width, 3 * feat_dev), preferred_element_type=jnp.float32
    ).reshape(tok_rows, 3, feat_dev)
    query_raw = projected[:, 0]
    key_raw = projected[:, 1]
    values_new = projected[:, 2].astype(jnp.bfloat16)
    query_total, key_total = lax.psum(
        (jnp.sum(query_raw * query_raw, axis=-1), jnp.sum(key_raw * key_raw, axis=-1)), TP
    )
    query_normed = query_raw * lax.rsqrt(query_total[:, None] / model_width + norm_eps) * qk_gain[0]
    key_normed = key_raw * lax.rsqrt(key_total[:, None] / model_width + norm_eps) * qk_gain[1]
    query_rot = rotate(query_normed.reshape(tok_rows, local_heads, HD), positions).astype(
        jnp.bfloat16
    )
    keys_new = rotate(key_normed.reshape(tok_rows, local_heads, HD), positions).astype(jnp.bfloat16)
    page_rows = kv_cache[:, page_table.reshape(-1)]
    context = page_table.shape[1] * kv_cache.shape[2]
    cache_keys = page_rows[0].reshape(req_local, context, local_heads, HD)
    cache_values = page_rows[1].reshape(req_local, context, local_heads, HD)
    query_blocks = query_rot.reshape(req_local, draft_len, local_heads, HD)
    key_blocks = keys_new.reshape(req_local, draft_len, local_heads, HD)
    value_blocks = values_new.reshape(req_local, draft_len, local_heads, HD)
    score_scale = HD ** (-0.5)
    cache_scores = (
        jnp.einsum("rjhd,rchd->rhjc", query_blocks, cache_keys, preferred_element_type=jnp.float32)
        * score_scale
    )
    live_keys = jnp.arange(context, dtype=jnp.int32)[None, :] < cache_lens[:, None]
    cache_scores = jnp.where(live_keys[:, None, None, :], cache_scores, masked_score)
    draft_scores = (
        jnp.einsum("rjhd,rihd->rhji", query_blocks, key_blocks, preferred_element_type=jnp.float32)
        * score_scale
    )
    draft_scores = jnp.where(ancestry[:, None, :, :] > 0.5, draft_scores, masked_score)
    scores = jnp.concatenate([cache_scores, draft_scores], axis=-1)
    row_max = jnp.max(scores, axis=-1, keepdims=True)
    weights = jnp.exp(scores - row_max)
    probabilities = (weights / jnp.sum(weights, axis=-1, keepdims=True)).astype(jnp.bfloat16)
    all_values = jnp.concatenate([cache_values, value_blocks], axis=1)
    attn_heads = (
        jnp.einsum("rhjc,rchd->rjhd", probabilities, all_values, preferred_element_type=jnp.float32)
        .astype(jnp.bfloat16)
        .reshape(tok_rows, feat_dev)
    )
    attn_term = jnp.dot(attn_heads, w_out, preferred_element_type=jnp.float32)
    residual = hidden.astype(jnp.float32) + lax.psum(attn_term, TP)
    normed_moe = rms_scale(residual, moe_gain).astype(jnp.bfloat16)
    residual_share = lax.dynamic_slice_in_dim(residual, slice_start, slice_width, 1)
    experts_here = EXPERTS // req_count
    tok_ids = jnp.arange(tok_rows, dtype=jnp.int32)
    route_hot = (routes[:, :, None] == jnp.arange(EXPERTS, dtype=jnp.int32)).astype(jnp.float32)
    per_token = jnp.sum(route_hot, axis=1)
    weight_of = jnp.sum(route_weights[:, :, None] * route_hot, axis=1)
    earlier = (tok_ids[:, None] > tok_ids[None, :]).astype(jnp.bfloat16)
    slot_of = jnp.dot(earlier, per_token.astype(jnp.bfloat16), preferred_element_type=jnp.float32)
    capacity = CAP
    cap_ids = jnp.arange(capacity, dtype=jnp.float32)
    picked_here = lax.dynamic_index_in_dim(
        per_token.reshape(tok_rows, req_count, experts_here), th, axis=2, keepdims=False
    ).T
    slot_here = lax.dynamic_index_in_dim(
        slot_of.reshape(tok_rows, req_count, experts_here), th, axis=2, keepdims=False
    ).T
    select = jnp.where(
        (picked_here[:, None, :] > 0.5) & (slot_here[:, None, :] == cap_ids[None, :, None]),
        1.0,
        0.0,
    ).astype(jnp.bfloat16)
    half_width = model_width // 2
    normed_half = lax.dynamic_slice_in_dim(normed_moe, tc * half_width, half_width, 1)
    send_rows = jnp.einsum(
        "ict,tw->icw", select, normed_half, preferred_element_type=jnp.float32
    ).astype(jnp.bfloat16)
    received = lax.all_to_all(send_rows, "req", 0, 0, tiled=True)
    rows = lax.all_gather(received, "tc", axis=2, tiled=True)
    gate_up = jnp.einsum("scw,wgu->scgu", rows, w_gate_up[0], preferred_element_type=jnp.float32)
    activated = (jax.nn.silu(gate_up[..., 0, :]) * gate_up[..., 1, :]).astype(jnp.bfloat16)
    units_dev = w_down.shape[1]
    down = w_down[0].reshape(units_dev, 2, 2, 2, slice_width)
    partial = jnp.einsum(
        "scu,uhlkd->shckld", activated, down, preferred_element_type=jnp.float32
    ).astype(jnp.bfloat16)
    partial = partial.reshape(req_count, 2, capacity, 4 * slice_width)
    partial = lax.psum_scatter(partial, "tc", scatter_dimension=3, tiled=True)
    partial = lax.psum_scatter(partial, "tl", scatter_dimension=3, tiled=True)
    back = partial.reshape(req_count * 2, capacity, slice_width)
    returned = lax.all_to_all(back, ("req", "th"), 0, 0, tiled=True)
    combine = weight_of[:, :, None] * (slot_of[:, :, None] == cap_ids[None, None, :])
    mixture = jnp.dot(
        combine.reshape(tok_rows, EXPERTS * capacity),
        returned.reshape(EXPERTS * capacity, slice_width).astype(jnp.float32),
        precision=lax.Precision.HIGHEST,
        preferred_element_type=jnp.float32,
    )
    output = (residual_share + mixture).astype(jnp.bfloat16)
    picked_rows = (jnp.arange(req_local, dtype=jnp.int32)[:, None] * draft_len + accepted).reshape(
        -1
    )
    accepted_kv = jnp.stack(
        [keys_new.reshape(tok_rows, feat_dev)[picked_rows], values_new[picked_rows]]
    )
    return (output, accepted_kv)


def solution(mesh):
    req_count = mesh.shape["req"]
    devices = mesh.devices.reshape(req_count, 2, 2, mesh.shape["tp"] // 4)
    split_mesh = Mesh(devices, ("req",) + TP)
    return jax.shard_map(
        local,
        mesh=split_mesh,
        in_specs=(
            P("req", None),
            P(None, "req", None, TP),
            P("req", None),
            P("req"),
            P("req", None),
            P("req", None),
            P(),
            P(None, None, TP),
            P(None, TP),
            P(TP, None),
            P(),
            P("req", None),
            P("req", None),
            P("req", None, None, TP),
            P("req", TP, None),
        ),
        out_specs=(P("req", TP), P(None, "req", TP)),
        check_vma=False,
    )
```

profile of v0, /device:TPU:32, one launch (start us, length us, event | category | flops | bytes accessed | tf_op | source)
XLA Modules:
  0.0 378.7 jit_solution(12945470743647845171)
XLA Ops:
  7.3 1.6 fusion.11
  8.9 4.8 %copy.67 = bf16[2048,3,256]{0,2,1:T(8,128)(2,1)} copy(bf16[2048,3,256]{2,0,1:T(8,128)(2,1)} %param.22) | data formatting | bytes 6291456 | tf_op args[7]
  13.8 3.0 fusion.2
  16.8 0.8 copy-done.6
  21.3 14.9 %all-reduce = (f32[256]{0:T(256)S(1)}, f32[256]{0:T(256)S(1)}) all-reduce(f32[256]{0:T(256)S(1)} %get-tuple-element.3, f32[256]{0:T(256)S(1)} %get-tuple-element.2), channel_id=1, replica_groups=mesh['req'=32,'th'=2,'tl'=2,'tc'=2] {'th','tl','tc'}, use_global_device_ids=true, to_apply=%region_5.0 | all-reduce | flops 512 | bytes 4096 | tf_op jit(solution)/shard_map/psum | solution.py:85
  37.1 0.8 copy.76
  39.0 0.8 copy.70
  39.8 4.9 %gather_fusion = bf16[32,2,128,256]{3,2,1,0:T(8,128)(2,1)} fusion(bf16[2,32,128,256]{3,2,1,0:T(8,128)(2,1)} %param.16, s32[1024]{0:T(1024)S(1)} %pad_clamp_fusion.1), kind=kCustom, calls=%fused_computation | custom fusion | bytes 8388736 | tf_op jit(solution)/shard_map/gather | solution.py:94
  44.7 4.7 %fusion.96 = (bf16[1,32,128,256]{3,2,0,1:T(8,128)(2,1)}, bf16[1,32,128,256]{3,2,0,1:T(8,128)(2,1)}) fusion(bf16[2,32,128,256]{3,2,0,1:T(8,128)(2,1)} %bitcast.107), kind=kLoop, calls=%fused_computation.138 | loop fusion | bytes 8388608 | tf_op jit(solution)/shard_map/slice | solution.py:96
  49.4 2.5 reshape_squeeze.10
  52.0 4.0 %reshape_squeeze.9 = bf16[4,1024,2,128]{3,2,1,0:T(2,128)(2,1)} reshape(bf16[1,32,128,256]{3,2,0,1:T(8,128)(2,1)} %get-tuple-element.11) | data formatting | bytes 4194304 | tf_op jit(solution)/shard_map/reshape;squeeze | solution.py:97
  55.9 1.9 copy.69
  57.8 1.0 fusion.99
  59.8 0.8 fusion.48
  60.8 1.8 fusion.70
  64.3 69.2 %all-reduce.3.cloned.1.call-done = f32[256,2048]{1,0:T(8,128)} async-done(((f32[256,2048]{1,0:T(8,128)}), f32[256,2048]{1,0:T(8,128)}) %all-reduce.3.cloned.1.call-update) | async-done | bytes 2097168 | tf_op jit(solution)/shard_map/psum | solution.py:124
  133.5 1.9 multiply_reduce_fusion
  135.5 1.0 convolution_convert_fusion
  136.5 70.3 %all_to_all.10 = bf16[32,40,1024]{2,1,0:T(8,128)(2,1)} all-to-all(bf16[32,40,1024]{2,1,0:T(8,128)(2,1)S(1)} %convolution_convert_fusion), channel_id=1, replica_groups=mesh['req'=32,'th'=2,'tl'=2,'tc'=2] {'req'}, dimensions={0} | all-to-all | bytes 5242880 | tf_op jit(solution)/shard_map/all_to_all | solution.py:152
  207.1 1.0 copy-done.4
  208.0 1.6 reshape_squeeze.11
  209.6 14.3 %all-gather.2.cloned.1.call-done = bf16[32,40,2048]{2,1,0:T(8,128)(2,1)} async-done(((bf16[32,40,1024]{2,1,0:T(8,128)(2,1)}), bf16[32,40,2048]{2,1,0:T(8,128)(2,1)}) %all-gather.2.cloned.1.call-update) | async-done | bytes 5242896 | tf_op jit(solution)/shard_map/all_gather | solution.py:153
  224.0 5.5 %fusion = f32[32,40,2,256]{3,1,2,0:T(8,128)S(1)} fusion(bf16[32,40,2048]{2,1,0:T(8,128)(2,1)} %all-gather.2.cloned.1.call-done, bf16[2048,2,256]{2,1,0:T(2,128)(2,1)} %bitcast.119), kind=kOutput, calls=%fused_computation.3 | convolution fusion | flops 2684354560 | bytes 9961472 | tf_op jit(solution)/shard_map/scw,wgu->scgu/dot_general | solution.py:154
  229.5 4.0 %convert_bitcast_fusion = bf16[32,2,40,2,2,256]{5,2,3,4,1,0:T(8,128)(2,1)} fusion(bf16[256,2,2,2,256]{4,3,2,1,0:T(2,128)(2,1)S(1)} %copy-done.5, f32[32,40,2,256]{3,1,2,0:T(8,128)S(1)} %fusion), kind=kOutput, calls=%fused_computation.5 | convolution fusion | flops 1346764800 | bytes 8912896 | tf_op jit(solution)/shard_map/scu,uhlkd->shckld/dot_general | solution.py:158
  233.5 10.3 %copy.81 = bf16[32,2,40,2,2,256]{5,4,3,2,1,0:T(2,128)(2,1)} copy(bf16[32,2,40,2,2,256]{5,2,3,4,1,0:T(8,128)(2,1)} %convert_bitcast_fusion) | data formatting | bytes 10485760 | tf_op jit(solution)/shard_map/convert_element_type | solution.py:160
  243.8 9.3 %reshape.284 = bf16[32,2,40,1024]{3,2,1,0:T(8,128)(2,1)} reshape(bf16[32,2,40,2,2,256]{5,4,3,2,1,0:T(2,128)(2,1)} %copy.81) | data formatting | bytes 10485760 | tf_op jit(solution)/shard_map/reshape | solution.py:161
  253.2 19.7 %reduce-scatter.3.cloned.1.call-done = bf16[32,2,40,512]{3,2,1,0:T(8,128)(2,1)} async-done(((bf16[32,2,40,1024]{3,2,1,0:T(8,128)(2,1)}), bf16[32,2,40,512]{3,2,1,0:T(8,128)(2,1)}) %reduce-scatter.3.cloned.1.call-update) | async-done | bytes 2621456 | tf_op jit(solution)/shard_map/reduce_scatter | solution.py:162
  273.0 46.4 %reduce-scatter.5.cloned.1.call-done = bf16[32,2,40,256]{3,2,1,0:T(8,128)(2,1)} async-done(((bf16[32,2,40,512]{3,2,1,0:T(8,128)(2,1)}), bf16[32,2,40,256]{3,2,1,0:T(8,128)(2,1)}) %reduce-scatter.5.cloned.1.call-update) | async-done | bytes 1310736 | tf_op jit(solution)/shard_map/reduce_scatter | solution.py:163
  319.4 12.8 %all-to-all-start.1 = ((bf16[64,40,256]{2,1,0:T(8,128)(2,1)}), bf16[64,40,256]{2,1,0:T(8,128)(2,1)}, u32[]{:S(2)}, u32[]{:S(2)}) async-start(bf16[64,40,256]{2,1,0:T(8,128)(2,1)} %bitcast.108), calls=%async_computation.3 | async-start | bytes 2621440 | tf_op jit(solution)/shard_map/all_to_all | solution.py:165
  332.2 1.0 slice_bitcast_fusion
  335.3 32.4 %all-to-all-done.1 = bf16[64,40,256]{2,1,0:T(8,128)(2,1)} async-done(((bf16[64,40,256]{2,1,0:T(8,128)(2,1)}), bf16[64,40,256]{2,1,0:T(8,128)(2,1)}, u32[]{:S(2)}, u32[]{:S(2)}) %all-to-all-start.1) | async-done | bytes 1310752 | tf_op jit(solution)/shard_map/all_to_all | solution.py:165
  367.7 4.4 %fusion.40 = bf16[256,256]{1,0:T(8,128)(2,1)} fusion(bf16[64,40,256]{2,1,0:T(8,128)(2,1)} %all-to-all-done.1, f32[256,64]{0,1:T(8,128)} %get-tuple-element.4, f32[256,64]{0,1:T(8,128)} %copy-done.9, f32[256,2048]{1,0:T(8,128)S(1)} %get-tuple-element.9, s32[]{:T(128)S(6)} %select_n.47), kind=kOutput, calls=%fused_computation.47 | convolution fusion | flops 2014707712 | bytes 1835012 | tf_op jit(solution)/shard_map/dot_general | solution.py:167
  (104 shorter events, 10.7 us)
Async XLA Ops:
  7.2 53.6 %copy-start = (bf16[256,2048]{1,0:T(8,128)(2,1)S(1)}, bf16[256,2048]{1,0:T(8,128)(2,1)}, u32[]{:S(2)}) copy-start(bf16[256,2048]{1,0:T(8,128)(2,1)} %param.24) | copy-start | bytes 3145732
  7.2 126.3 %all-reduce.3.cloned.1.call-start = ((), (), s32[]{:S(2)}) async-start(), calls=%async_computation.4 | async-start | bytes 4194304 | tf_op jit(solution)/shard_map/psum | solution.py:124
  8.9 4.9 %copy-start.2 = (bf16[256,2048]{1,0:T(8,128)(2,1)S(1)}, bf16[256,2048]{1,0:T(8,128)(2,1)}, u32[]{:S(2)}) copy-start(bf16[256,2048]{1,0:T(8,128)(2,1)} %param.15) | copy-start | bytes 3145732
  8.9 4.9 %copy-start.19 = (f32[2048]{0:T(1024)S(1)}, f32[2048]{0:T(1024)}, u32[]{:S(2)}) copy-start(f32[2048]{0:T(1024)} %param.21) | copy-start | bytes 24580
  13.7 4.0 %copy-start.15 = (s32[4,8]{1,0:T(4,128)S(1)}, s32[4,8]{1,0:T(4,128)}, u32[]{:S(2)}) copy-start(s32[4,8]{1,0:T(4,128)} %param.17) | copy-start | bytes 388
  13.7 4.1 %copy-start.16 = (s32[4,8]{1,0:T(4,128)S(1)}, s32[4,8]{1,0:T(4,128)}, u32[]{:S(2)}) copy-start(s32[4,8]{1,0:T(4,128)} %param.20) | copy-start | bytes 388
  13.7 4.2 %copy-start.17 = (f32[2,256]{1,0:T(2,128)S(1)}, f32[2,256]{1,0:T(2,128)}, u32[]{:S(2)}) copy-start(f32[2,256]{1,0:T(2,128)} %param.23) | copy-start | bytes 6148
  13.8 4.3 %copy-start.14 = (s32[4]{0:T(128)S(1)}, s32[4]{0:T(128)}, u32[]{:S(2)}) copy-start(s32[4]{0:T(128)} %param.18) | copy-start | bytes 52
  13.8 4.3 %copy-start.18 = (s32[4,64]{1,0:T(4,128)S(1)}, s32[4,64]{1,0:T(4,128)}, u32[]{:S(2)}) copy-start(s32[4,64]{1,0:T(4,128)} %param.19) | copy-start | bytes 3076
  16.8 0.9 copy-start.6
  57.8 1.0 copy-start.7
  57.8 1.0 copy-start.8
  57.8 1.0 copy-start.11
  58.9 0.9 copy-start.10
  60.8 1.9 copy-start.12
  60.8 1.9 copy-start.13
  62.5 71.0 %copy-start.3 = (bf16[256,2048]{1,0:T(8,128)(2,1)S(1)}, bf16[256,2048]{1,0:T(8,128)(2,1)}, u32[]{:S(2)}) copy-start(bf16[256,2048]{1,0:T(8,128)(2,1)} %param.15) | copy-start | bytes 3145732
  62.6 161.4 %all-gather.2.cloned.1.call-start = ((), (), s32[]{:S(2)}) async-start(), calls=%async_computation.5 | async-start | bytes 7864320 | tf_op jit(solution)/shard_map/all_gather | solution.py:153
  63.6 0.6 copy-start.9
  64.3 71.2 %dynamic-slice-start = ((f32[2048]{0:T(1024)}, s32[]{:T(128)}), f32[1024]{0:T(1024)S(1)}, s32[]{:S(2)}) async-start(f32[2048]{0:T(1024)} %param.25, s32[]{:T(128)} %select_n.50), calls=%async_computation.8 | async-start | bytes 8704 | tf_op jit(solution)/shard_map/dynamic_slice | solution.py:148
  206.8 1.2 copy-start.4
  206.8 66.1 %reduce-scatter.3.cloned.1.call-start = ((), (), s32[]{:S(2)}) async-start(), calls=%async_computation.6 | async-start | bytes 7864320 | tf_op jit(solution)/shard_map/reduce_scatter | solution.py:162
  224.0 5.5 %copy-start.5 = (bf16[256,2,2,2,256]{4,3,2,1,0:T(2,128)(2,1)S(1)}, bf16[256,2,2,2,256]{4,3,2,1,0:T(2,128)(2,1)}, u32[]{:S(2)}) copy-start(bf16[256,2,2,2,256]{4,3,2,1,0:T(2,128)(2,1)} %reshape_squeeze.11) | copy-start | bytes 3145732
  253.2 66.2 %reduce-scatter.5.cloned.1.call-start = ((), (), s32[]{:S(2)}) async-start(), calls=%async_computation.7 | async-start | bytes 3932160 | tf_op jit(solution)/shard_map/reduce_scatter | solution.py:163
  319.4 48.3 %all-to-all-start.1 = ((bf16[64,40,256]{2,1,0:T(8,128)(2,1)}), bf16[64,40,256]{2,1,0:T(8,128)(2,1)}, u32[]{:S(2)}, u32[]{:S(2)}) async-start(bf16[64,40,256]{2,1,0:T(8,128)(2,1)} %bitcast.108), calls=%async_computation.3 | async-start | bytes 2621440 | tf_op jit(solution)/shard_map/all_to_all | solution.py:165
  367.7 4.4 %copy-start.1 = (bf16[256,2048]{1,0:T(8,128)(2,1)S(1)}, bf16[256,2048]{1,0:T(8,128)(2,1)}, u32[]{:S(2)}) copy-start(bf16[256,2048]{1,0:T(8,128)(2,1)} %param.24) | copy-start | bytes 3145732
Sparse Core Ops, SparseCore 0:
  62.7 70.7 all-reduce.2
  206.9 16.9 all-gather.1
  253.3 19.5 reduce-scatter.2
  275.3 44.0 reduce-scatter.4
where the time goes:
time: 380 us; the launch traced here: 379 us
  waiting for transfers between devices  182 us (48%)
  blocking collectives  85.2 us (22%)
  local copies, waits for them, and re-layouts  52.8 us (14%)
  matrix products  24.1 us (6%)
  between operations  14.3 us (4%)
  starting transfers between devices  13.1 us (3%)
  other arithmetic  7 us (2%)
    all_to_all x1, blocking collectives, local(): received = lax.all_to_all(send_rows, 'req', 0, 0, tiled=True)  70.3 us
    psum x1, waiting for transfers between devices, local(): residual = hidden.astype(jnp.float32) + lax.psum(attn_term, TP)  69.2 us
    reduce_scatter x1, waiting for transfers between devices, local(): partial = lax.psum_scatter(partial, 'tl', scatter_dimension=3, tiled=True)  46.4 us
    all_to_all x1, waiting for transfers between devices, local(): returned = lax.all_to_all(back, ('req', 'th'), 0, 0, tiled=True)  32.4 us
    reduce_scatter x1, waiting for transfers between devices, local(): partial = lax.psum_scatter(partial, 'tc', scatter_dimension=3, tiled=True)  19.7 us
    psum x1, blocking collectives, local(): lax.psum((jnp.sum(query_raw * query_raw, axis=-1), jnp.sum(key_raw * key_...  14.9 us
    all_gather x1, waiting for transfers between devices, local(): rows = lax.all_gather(received, 'tc', axis=2, tiled=True)  14.3 us
    all_to_all x1, starting transfers between devices, local(): returned = lax.all_to_all(back, ('req', 'th'), 0, 0, tiled=True)  12.8 us
  transfers between devices with their start and end apart: 5, of which 5 were waited for; matrix products, arithmetic and copies ran while one was open for 2% of the time, Pallas kernels for 0%

commit v1 on v0

--- a/solution.py
+++ b/solution.py
@@ -62,6 +62,12 @@
     w_gate_up,
     w_down,
 ):
+
+    def row_point(target, array_dim=2):
+        s_next = jnp.stack([target for _ in range(lax.axis_size("tc"))])
+        z_new = lax.all_to_all(s_next, axis_name="tc", split_axis=0, concat_axis=0)
+        return jnp.concatenate(z_new, axis=array_dim)
+
     tok_rows, model_width = hidden.shape
     th = lax.axis_index("th")
     tl = lax.axis_index("tl")
@@ -150,7 +156,7 @@
         "ict,tw->icw", select, normed_half, preferred_element_type=jnp.float32
     ).astype(jnp.bfloat16)
     received = lax.all_to_all(send_rows, "req", 0, 0, tiled=True)
-    rows = lax.all_gather(received, "tc", axis=2, tiled=True)
+    rows = row_point(received)
     gate_up = jnp.einsum("scw,wgu->scgu", rows, w_gate_up[0], preferred_element_type=jnp.float32)
     activated = (jax.nn.silu(gate_up[..., 0, :]) * gate_up[..., 1, :]).astype(jnp.bfloat16)
     units_dev = w_down.shape[1]

time: 380 us -> 396 us (1.042)
  blocking collectives: 85.2 us -> 23.9 us
  waiting for transfers between devices: 182 us -> 223 us
  local copies, waits for them, and re-layouts: 52.8 us -> 75.5 us
  starting transfers between devices: 13.1 us -> 23.1 us
    all_to_all x1, blocking collectives: 70.3 us -> 9.06 us  [row_point(): z_new = lax.all_to_all(s_next, axis_name='tc', split_axis=0, concat_axis=0)]
    all_to_all x0 -> x1, waiting for transfers between devices: none -> 57.4 us  [local(): received = lax.all_to_all(send_rows, 'req', 0, 0, tiled=True)]
    reshape x0 -> x2, local copies, waits for them, and re-layouts: none -> 19.6 us  [row_point(): return jnp.concatenate(z_new, axis=array_dim)]
    all_gather x1 -> x0, waiting for transfers between devices: 14.3 us -> none  [local(): rows = lax.all_gather(received, 'tc', axis=2, tiled=True)]
    all_to_all x0 -> x1, starting transfers between devices: none -> 10.2 us  [local(): received = lax.all_to_all(send_rows, 'req', 0, 0, tiled=True)]
  transfers between devices with their start and end apart: 5 -> 5, of which waited for: 5 -> 5; matrix products, arithmetic and copies ran while one was open for 2% -> 1% of each run, Pallas kernels for 0% -> 0%
where the time goes in v1:
time: 396 us; the launch traced here: 395 us
  waiting for transfers between devices  223 us (56%)
  local copies, waits for them, and re-layouts  75.5 us (19%)
  matrix products  25.7 us (6%)
  blocking collectives  23.9 us (6%)
  starting transfers between devices  23.1 us (6%)
  between operations  14.3 us (4%)
  other arithmetic  8.73 us (2%)
    psum x1, waiting for transfers between devices, local(): residual = hidden.astype(jnp.float32) + lax.psum(attn_term, TP)  69.8 us
    all_to_all x1, waiting for transfers between devices, local(): received = lax.all_to_all(send_rows, 'req', 0, 0, tiled=True)  57.4 us
    reduce_scatter x1, waiting for transfers between devices, local(): partial = lax.psum_scatter(partial, 'tl', scatter_dimension=3, tiled=True)  46.5 us
    all_to_all x1, waiting for transfers between devices, local(): returned = lax.all_to_all(back, ('req', 'th'), 0, 0, tiled=True)  32.4 us
    reshape x2, local copies, waits for them, and re-layouts, row_point(): return jnp.concatenate(z_new, axis=array_dim)  19.6 us
    reduce_scatter x1, waiting for transfers between devices, local(): partial = lax.psum_scatter(partial, 'tc', scatter_dimension=3, tiled=True)  17.2 us
    psum x1, blocking collectives, local(): lax.psum((jnp.sum(query_raw * query_raw, axis=-1), jnp.sum(key_raw * key_...  14.8 us
    all_to_all x1, starting transfers between devices, local(): returned = lax.all_to_all(back, ('req', 'th'), 0, 0, tiled=True)  12.8 us
  transfers between devices with their start and end apart: 5, of which 5 were waited for; matrix products, arithmetic and copies ran while one was open for 1% of the time, Pallas kernels for 0%

profile of v1, /device:TPU:32, one launch (start us, length us, event | category | flops | bytes accessed | tf_op | source)
XLA Modules:
  0.0 394.6 jit_solution(8432448749137148182)
XLA Ops:
  7.3 4.9 %copy.89 = bf16[2048,3,256]{0,2,1:T(8,128)(2,1)} copy(bf16[2048,3,256]{2,0,1:T(8,128)(2,1)} %param.22) | data formatting | bytes 6291456 | tf_op args[7]
  12.5 3.0 fusion.2
  18.8 14.8 %all-reduce = (f32[256]{0:T(256)S(1)}, f32[256]{0:T(256)S(1)}) all-reduce(f32[256]{0:T(256)S(1)} %get-tuple-element.3, f32[256]{0:T(256)S(1)} %get-tuple-element.2), channel_id=1, replica_groups=mesh['req'=32,'th'=2,'tl'=2,'tc'=2] {'th','tl','tc'}, use_global_device_ids=true, to_apply=%region_5.0 | all-reduce | flops 512 | bytes 4096 | tf_op jit(solution)/shard_map/psum | solution.py:91
  37.5 4.9 %gather_fusion = bf16[32,2,128,256]{3,2,1,0:T(8,128)(2,1)} fusion(bf16[2,32,128,256]{3,2,1,0:T(8,128)(2,1)} %param.16, s32[1024]{0:T(1024)S(1)} %pad_clamp_fusion.1), kind=kCustom, calls=%fused_computation | custom fusion | bytes 8388736 | tf_op jit(solution)/shard_map/gather | solution.py:100
  42.4 4.7 %fusion.96 = (bf16[1,32,128,256]{3,2,0,1:T(8,128)(2,1)}, bf16[1,32,128,256]{3,2,0,1:T(8,128)(2,1)}) fusion(bf16[2,32,128,256]{3,2,0,1:T(8,128)(2,1)} %bitcast.108), kind=kLoop, calls=%fused_computation.139 | loop fusion | bytes 8388608 | tf_op jit(solution)/shard_map/slice | solution.py:102
  47.1 2.5 reshape_squeeze.10
  49.7 4.0 %reshape_squeeze.9 = bf16[4,1024,2,128]{3,2,1,0:T(2,128)(2,1)} reshape(bf16[1,32,128,256]{3,2,0,1:T(8,128)(2,1)} %get-tuple-element.11) | data formatting | bytes 4194304 | tf_op jit(solution)/shard_map/reshape;squeeze | solution.py:103
  53.6 3.2 copy.91
  56.8 1.8 reshape.326
  58.6 1.7 copy.92
  60.4 1.0 fusion.99
  64.0 1.8 fusion.70
  66.9 69.8 %all-reduce.3.cloned.1.call-done = f32[256,2048]{1,0:T(8,128)} async-done(((f32[256,2048]{1,0:T(8,128)}), f32[256,2048]{1,0:T(8,128)}) %all-reduce.3.cloned.1.call-update) | async-done | bytes 2097168 | tf_op jit(solution)/shard_map/psum | solution.py:130
  136.7 1.9 multiply_reduce_fusion
  138.7 2.5 convolution_convert_fusion
  141.2 10.2 %all-to-all-start = ((bf16[32,40,1024]{2,1,0:T(8,128)(2,1)}), bf16[32,40,1024]{2,1,0:T(8,128)(2,1)}, u32[]{:S(2)}, u32[]{:S(2)}) async-start(bf16[32,40,1024]{2,1,0:T(8,128)(2,1)} %convolution_convert_fusion), calls=%async_computation | async-start | bytes 5242880 | tf_op jit(solution)/shard_map/all_to_all | solution.py:158
  151.5 1.6 reshape_squeeze.11
  153.1 57.4 %all-to-all-done = bf16[32,40,1024]{2,1,0:T(8,128)(2,1)} async-done(((bf16[32,40,1024]{2,1,0:T(8,128)(2,1)}), bf16[32,40,1024]{2,1,0:T(8,128)(2,1)}, u32[]{:S(2)}, u32[]{:S(2)}) %all-to-all-start) | async-done | bytes 2621472 | tf_op jit(solution)/shard_map/all_to_all | solution.py:158
  210.5 3.0 pad_maximum_fusion
  213.5 9.1 %all_to_all.15 = bf16[2,32,40,1024]{3,2,1,0:T(8,128)(2,1)} all-to-all(bf16[2,32,40,1024]{3,2,1,0:T(8,128)(2,1)S(1)} %pad_maximum_fusion), channel_id=1, replica_groups=mesh['req'=32,'th'=2,'tl'=2,'tc'=2] {'tc'}, dimensions={0} | all-to-all | bytes 10485760 | tf_op jit(solution)/shard_map/all_to_all | solution.py:68
  222.6 10.2 %copy.101 = bf16[32,40,2,1024]{3,2,1,0:T(2,128)(2,1)} copy(bf16[32,40,2,1024]{3,1,0,2:T(8,128)(2,1)} %bitcast.107) | data formatting | bytes 10485760 | tf_op jit(solution)/shard_map/reshape | solution.py:69
  232.7 9.4 %reshape.321 = bf16[32,40,2048,1]{2,1,0,3:T(8,128)(2,1)} reshape(bf16[32,40,2,1024]{3,2,1,0:T(2,128)(2,1)} %copy.101) | data formatting | bytes 10485760 | tf_op jit(solution)/shard_map/reshape | solution.py:69
  242.2 5.8 %fusion = f32[32,40,2,256]{3,1,2,0:T(8,128)S(1)} fusion(bf16[32,40,2048,1]{2,1,0,3:T(8,128)(2,1)} %reshape.321, bf16[2048,2,256]{2,1,0:T(2,128)(2,1)} %bitcast.120), kind=kOutput, calls=%fused_computation.4 | convolution fusion | flops 2684354560 | bytes 9961472 | tf_op jit(solution)/shard_map/scw,wgu->scgu/dot_general | solution.py:160
  247.9 4.0 %convert_bitcast_fusion = bf16[32,2,40,2,2,256]{5,2,3,4,1,0:T(8,128)(2,1)} fusion(bf16[256,2,2,2,256]{4,3,2,1,0:T(2,128)(2,1)S(1)} %copy-done.6, f32[32,40,2,256]{3,1,2,0:T(8,128)S(1)} %fusion), kind=kOutput, calls=%fused_computation.6 | convolution fusion | flops 1346764800 | bytes 8912896 | tf_op jit(solution)/shard_map/scu,uhlkd->shckld/dot_general | solution.py:164
  251.9 10.3 %copy.104 = bf16[32,2,40,2,2,256]{5,4,3,2,1,0:T(2,128)(2,1)} copy(bf16[32,2,40,2,2,256]{5,2,3,4,1,0:T(8,128)(2,1)} %convert_bitcast_fusion) | data formatting | bytes 10485760 | tf_op jit(solution)/shard_map/convert_element_type | solution.py:166
  262.3 9.3 %reshape.292 = bf16[32,2,40,1024]{3,2,1,0:T(8,128)(2,1)} reshape(bf16[32,2,40,2,2,256]{5,4,3,2,1,0:T(2,128)(2,1)} %copy.104) | data formatting | bytes 10485760 | tf_op jit(solution)/shard_map/reshape | solution.py:167
  271.7 17.2 %reduce-scatter.3.cloned.1.call-done = bf16[32,2,40,512]{3,2,1,0:T(8,128)(2,1)} async-done(((bf16[32,2,40,1024]{3,2,1,0:T(8,128)(2,1)}), bf16[32,2,40,512]{3,2,1,0:T(8,128)(2,1)}) %reduce-scatter.3.cloned.1.call-update) | async-done | bytes 2621456 | tf_op jit(solution)/shard_map/reduce_scatter | solution.py:168
  288.9 46.5 %reduce-scatter.5.cloned.1.call-done = bf16[32,2,40,256]{3,2,1,0:T(8,128)(2,1)} async-done(((bf16[32,2,40,512]{3,2,1,0:T(8,128)(2,1)}), bf16[32,2,40,256]{3,2,1,0:T(8,128)(2,1)}) %reduce-scatter.5.cloned.1.call-update) | async-done | bytes 1310736 | tf_op jit(solution)/shard_map/reduce_scatter | solution.py:169
  335.4 12.8 %all-to-all-start.2 = ((bf16[64,40,256]{2,1,0:T(8,128)(2,1)}), bf16[64,40,256]{2,1,0:T(8,128)(2,1)}, u32[]{:S(2)}, u32[]{:S(2)}) async-start(bf16[64,40,256]{2,1,0:T(8,128)(2,1)} %bitcast.109), calls=%async_computation.4 | async-start | bytes 2621440 | tf_op jit(solution)/shard_map/all_to_all | solution.py:171
  348.3 1.0 slice_bitcast_fusion
  351.3 32.4 %all-to-all-done.2 = bf16[64,40,256]{2,1,0:T(8,128)(2,1)} async-done(((bf16[64,40,256]{2,1,0:T(8,128)(2,1)}), bf16[64,40,256]{2,1,0:T(8,128)(2,1)}, u32[]{:S(2)}, u32[]{:S(2)}) %all-to-all-start.2) | async-done | bytes 1310752 | tf_op jit(solution)/shard_map/all_to_all | solution.py:171
  383.7 4.4 %fusion.40 = bf16[256,256]{1,0:T(8,128)(2,1)} fusion(bf16[64,40,256]{2,1,0:T(8,128)(2,1)} %all-to-all-done.2, f32[256,64]{0,1:T(8,128)S(1)} %copy-done.12, f32[256,64]{0,1:T(8,128)S(1)} %fusion.69, f32[256,2048]{1,0:T(8,128)S(1)} %get-tuple-element.9, s32[]{:T(128)S(6)} %select_n.47), kind=kOutput, calls=%fused_computation.48 | convolution fusion | flops 2014707712 | bytes 1835012 | tf_op jit(solution)/shard_map/dot_general | solution.py:173
  (108 shorter events, 13.2 us)
Async XLA Ops:
  7.2 56.8 %copy-start = (bf16[256,2048]{1,0:T(8,128)(2,1)S(1)}, bf16[256,2048]{1,0:T(8,128)(2,1)}, u32[]{:S(2)}) copy-start(bf16[256,2048]{1,0:T(8,128)(2,1)} %param.24) | copy-start | bytes 3145732
  7.2 129.5 %all-reduce.3.cloned.1.call-start = ((), (), s32[]{:S(2)}) async-start(), calls=%async_computation.5 | async-start | bytes 4194304 | tf_op jit(solution)/shard_map/psum | solution.py:130
  7.3 4.9 %copy-start.2 = (bf16[256,2048]{1,0:T(8,128)(2,1)S(1)}, bf16[256,2048]{1,0:T(8,128)(2,1)}, u32[]{:S(2)}) copy-start(bf16[256,2048]{1,0:T(8,128)(2,1)} %param.15) | copy-start | bytes 3145732
  7.3 5.2 %copy-start.20 = (f32[2048]{0:T(1024)S(1)}, f32[2048]{0:T(1024)}, u32[]{:S(2)}) copy-start(f32[2048]{0:T(1024)} %param.21) | copy-start | bytes 24580
  12.5 3.9 copy-start.17
  12.5 3.9 copy-start.19
  15.5 3.0 copy-start.7
  15.5 3.0 copy-start.15
  18.5 18.7 %copy-start.18 = (s32[4,8]{1,0:T(4,128)S(1)}, s32[4,8]{1,0:T(4,128)}, u32[]{:S(2)}) copy-start(s32[4,8]{1,0:T(4,128)} %param.20) | copy-start | bytes 388
  18.5 18.8 %copy-start.16 = (s32[4,8]{1,0:T(4,128)S(1)}, s32[4,8]{1,0:T(4,128)}, u32[]{:S(2)}) copy-start(s32[4,8]{1,0:T(4,128)} %param.17) | copy-start | bytes 388
  60.4 1.0 copy-start.8
  60.4 1.0 copy-start.9
  60.4 1.0 copy-start.11
  61.4 1.6 copy-start.4
  61.4 1.6 copy-start.10
  63.9 1.8 copy-start.13
  64.0 1.8 copy-start.14
  65.7 71.0 %copy-start.3 = (bf16[256,2048]{1,0:T(8,128)(2,1)S(1)}, bf16[256,2048]{1,0:T(8,128)(2,1)}, u32[]{:S(2)}) copy-start(bf16[256,2048]{1,0:T(8,128)(2,1)} %param.15) | copy-start | bytes 3145732
  66.9 71.7 %dynamic-slice-start = ((f32[2048]{0:T(1024)}, s32[]{:T(128)}), f32[1024]{0:T(1024)S(1)}, s32[]{:S(2)}) async-start(f32[2048]{0:T(1024)} %param.25, s32[]{:T(128)} %select_n.50), calls=%async_computation.8 | async-start | bytes 8704 | tf_op jit(solution)/shard_map/dynamic_slice | solution.py:154
  141.2 10.3 %copy-start.5 = (bf16[1,256,2048]{2,1,0:T(8,128)(2,1)S(1)}, bf16[1,256,2048]{2,1,0:T(8,128)(2,1)}, u32[]{:S(2)}) copy-start(bf16[1,256,2048]{2,1,0:T(8,128)(2,1)} %param.29) | copy-start | bytes 3145732
  141.2 69.3 %all-to-all-start = ((bf16[32,40,1024]{2,1,0:T(8,128)(2,1)}), bf16[32,40,1024]{2,1,0:T(8,128)(2,1)}, u32[]{:S(2)}, u32[]{:S(2)}) async-start(bf16[32,40,1024]{2,1,0:T(8,128)(2,1)} %convolution_convert_fusion), calls=%async_computation | async-start | bytes 5242880 | tf_op jit(solution)/shard_map/all_to_all | solution.py:158
  151.4 137.4 %reduce-scatter.3.cloned.1.call-start = ((), (), s32[]{:S(2)}) async-start(), calls=%async_computation.6 | async-start | bytes 7864320 | tf_op jit(solution)/shard_map/reduce_scatter | solution.py:168
  242.2 5.8 %copy-start.6 = (bf16[256,2,2,2,256]{4,3,2,1,0:T(2,128)(2,1)S(1)}, bf16[256,2,2,2,256]{4,3,2,1,0:T(2,128)(2,1)}, u32[]{:S(2)}) copy-start(bf16[256,2,2,2,256]{4,3,2,1,0:T(2,128)(2,1)} %reshape_squeeze.11) | copy-start | bytes 3145732
  271.6 63.8 %reduce-scatter.5.cloned.1.call-start = ((), (), s32[]{:S(2)}) async-start(), calls=%async_computation.7 | async-start | bytes 3932160 | tf_op jit(solution)/shard_map/reduce_scatter | solution.py:169
  288.9 94.9 %copy-start.12 = (f32[256,64]{0,1:T(8,128)S(1)}, f32[256,64]{0,1:T(8,128)}, u32[]{:S(2)}) copy-start(f32[256,64]{0,1:T(8,128)} %get-tuple-element.4) | copy-start | bytes 196612
  335.4 48.3 %all-to-all-start.2 = ((bf16[64,40,256]{2,1,0:T(8,128)(2,1)}), bf16[64,40,256]{2,1,0:T(8,128)(2,1)}, u32[]{:S(2)}, u32[]{:S(2)}) async-start(bf16[64,40,256]{2,1,0:T(8,128)(2,1)} %bitcast.109), calls=%async_computation.4 | async-start | bytes 2621440 | tf_op jit(solution)/shard_map/all_to_all | solution.py:171
  383.7 4.4 %copy-start.1 = (bf16[256,2048]{1,0:T(8,128)(2,1)S(1)}, bf16[256,2048]{1,0:T(8,128)(2,1)}, u32[]{:S(2)}) copy-start(bf16[256,2048]{1,0:T(8,128)(2,1)} %param.24) | copy-start | bytes 3145732
Sparse Core Ops, SparseCore 0:
  65.9 70.7 all-reduce.2
  271.7 17.0 reduce-scatter.2
  291.3 44.0 reduce-scatter.4
